TPU v7x, 32 devices: a whole 2x2x4 slice. The times are simulated.
32 devices in a mesh: grp: 8 (over y, x, core), ent: 4 (over z).
Axes of the slice: x: 2, y: 2, z: 4, core: 2. Of those that a mesh axis runs over, the one named last changes fastest.
Arguments:
- factor: bfloat16 [4096, 256], P(('grp', 'ent')), may hold values from -1.5 to 1.5
- cores: bfloat16 [16, 256, 256], replicated, may hold values from -0.375 to 0.375
- adjacency: int32 [768, 128, 128], P(('grp', 'ent')), may hold values 0 or 1
- tile_rels: int32 [32, 24], P(('grp', 'ent')), may hold values from 0 to 15
- tile_count: int32 [32], P(('grp', 'ent')), may hold values from 1 to 24, 480 in all
- send_lists: int32 [32, 4, 6], P(('grp', 'ent')), may hold values from 0 to 7
Outputs:
- factor_grad: float32 [4096, 256], P(('grp', 'ent'))
All inputs are finite; a program needn't handle non-finite values. No bound on the sum of `adjacency` or of `tile_count` on one device may be relied on, other than what follows from the above.
Results may differ from a plain program's by a relative error of at most 0.002.
Values may be sent and summed in bfloat16 or wider, within the bound.
No kernel may reach another device: no remote copies, remote signals or barrier semaphores. Data moves between devices by JAX's collectives and lax.ppermute only.
A program may use at most 64 MiB of HBM per device.

v0:
```python
import jax
import jax.numpy as jnp
from jax import lax
from jax.sharding import PartitionSpec as P

LOSS_SCALE = 0.0625


def on_device(factor, cores, adjacency, tile_rels, tile_count, send_lists):
    ent_count = lax.axis_size("ent")
    grp_count = lax.axis_size("grp")
    my_ent = lax.axis_index("ent")
    tiles = tile_rels.shape[1]
    block = factor.shape[0]
    width = factor.shape[1]
    per_relay = tiles // ent_count
    slots = ent_count * per_relay
    relations = tile_rels[0]
    routes = send_lists[0].reshape(slots)
    group_blocks = lax.all_gather(factor[None], "grp", axis=0, tiled=True)
    outgoing = group_blocks[routes].reshape(ent_count, per_relay, block, width)
    arrived = lax.all_to_all(outgoing, "ent", split_axis=0, concat_axis=0, tiled=True).reshape(
        slots, block, width
    )
    tile_ids = jnp.arange(tiles, dtype=jnp.int32)
    slot_of_tile = (my_ent + tile_ids) % ent_count * per_relay + tile_ids // ent_count
    factor_panels = arrived[slot_of_tile]
    live = (tile_ids < tile_count[0]).astype(jnp.float32)
    by_relation = jnp.einsum(
        "br,krs->kbs", factor, cores, preferred_element_type=jnp.float32
    ).astype(jnp.bfloat16)
    mapped_tiles = by_relation[relations]
    predicted_scores = jnp.einsum(
        "ogj,omj->ogm", mapped_tiles, factor_panels, preferred_element_type=jnp.float32
    )
    score_residual = (
        (predicted_scores - adjacency.astype(jnp.float32)) * (LOSS_SCALE * live)[:, None, None]
    ).astype(jnp.bfloat16)
    relation_product = jnp.einsum(
        "xmw,xwe->xme", score_residual, factor_panels, preferred_element_type=jnp.float32
    ).astype(jnp.bfloat16)
    row_grad = jnp.einsum(
        "tbs,trs->br", relation_product, cores[relations], preferred_element_type=jnp.float32
    )
    slot_ids = jnp.arange(slots, dtype=jnp.int32)
    tile_of_slot = slot_ids % per_relay * ent_count + (slot_ids // per_relay - my_ent) % ent_count
    column_terms = jnp.einsum(
        "yzj,yzh->yjh", score_residual, mapped_tiles, preferred_element_type=jnp.float32
    ).astype(jnp.bfloat16)
    sent_terms = column_terms[tile_of_slot].reshape(ent_count, per_relay, block, width)
    returned = (
        lax.all_to_all(sent_terms, "ent", split_axis=0, concat_axis=0, tiled=True)
        .reshape(slots, block * width)
        .astype(jnp.float32)
    )
    owner_onehot = (routes[:, None] == jnp.arange(grp_count, dtype=jnp.int32)[None, :]).astype(
        jnp.float32
    )
    owner_terms = jnp.dot(
        owner_onehot.T,
        returned,
        precision=lax.Precision.HIGHEST,
        preferred_element_type=jnp.float32,
    )
    owner_part = lax.psum_scatter(
        owner_terms.reshape(grp_count, block, width), "grp", scatter_dimension=0, tiled=True
    )
    return row_grad + owner_part[0]


def solution(mesh):
    in_specs = (
        P(("grp", "ent"), None),
        P(),
        P(("grp", "ent"), None, None),
        P(("grp", "ent"), None),
        P(("grp", "ent")),
        P(("grp", "ent"), None, None),
    )
    out_specs = P(("grp", "ent"), None)
    return jax.shard_map(
        on_device, mesh=mesh, in_specs=in_specs, out_specs=out_specs, check_vma=False
    )
```

profile of v0, /device:TPU:0, one launch (start us, length us, event | category | flops | bytes accessed | tf_op | source)
XLA Modules:
  0.0 166.0 jit_solution(857811333616795226)
XLA Ops:
  6.5 0.0 copy-start
  6.5 0.9 reshape_squeeze.3
  7.5 11.6 %all-gather = bf16[1024,256]{1,0:T(8,128)(2,1)S(1)} all-gather(bf16[128,256]{1,0:T(8,128)(2,1)} %param.6), channel_id=2, replica_groups=mesh['grp'=8,'ent'=4] {'grp'}, dimensions={0}, use_global_device_ids=true | all-gather | bytes 589824 | tf_op jit(solution)/shard_map/all_gather | solution.py:20
  19.1 1.9 %gather_fusion.1 = bf16[24,128,256]{2,1,0:T(8,128)(2,1)} fusion(bf16[8,128,256]{2,1,0:T(8,128)(2,1)S(1)} %bitcast.50, s32[1024]{0:T(1024)S(1)} %pad_clamp_fusion.2), kind=kCustom, calls=%fused_computation.1 | custom fusion | bytes 3145824 | tf_op jit(solution)/shard_map/gather | solution.py:21
  20.9 0.0 copy-start.4
  20.9 0.0 copy-start.2
  20.9 5.0 %all-to-all-start = ((bf16[4,6,128,256]{3,2,1,0:T(8,128)(2,1)}), bf16[4,6,128,256]{3,2,1,0:T(8,128)(2,1)}, u32[]{:S(2)}, u32[]{:S(2)}) async-start(bf16[4,6,128,256]{3,2,1,0:T(8,128)(2,1)} %bitcast.51), calls=%async_computation | async-start | bytes 3145728 | tf_op jit(solution)/shard_map/all_to_all | solution.py:22
  26.6 0.0 copy-done.4
  26.6 0.0 copy-done
  26.6 0.0 copy-done.2
  26.6 0.8 fusion.4
  27.4 1.9 %gather_fusion = bf16[24,128,256]{1,2,0:T(8,128)(2,1)} fusion(bf16[16,128,256]{1,2,0:T(8,128)(2,1)S(1)} %fusion.4, s32[1024]{0:T(1024)S(1)} %pad_clamp_fusion.3), kind=kCustom, calls=%fused_computation | custom fusion | bytes 3145824 | tf_op jit(solution)/shard_map/gather | solution.py:32
  29.4 34.1 %all-to-all-done = bf16[4,6,128,256]{3,2,1,0:T(8,128)(2,1)} async-done(((bf16[4,6,128,256]{3,2,1,0:T(8,128)(2,1)}), bf16[4,6,128,256]{3,2,1,0:T(8,128)(2,1)}, u32[]{:S(2)}, u32[]{:S(2)}) %all-to-all-start) | async-done | bytes 1572896 | tf_op jit(solution)/shard_map/all_to_all | solution.py:22
  63.5 3.3 %gather_fusion.2 = bf16[24,128,256]{2,1,0:T(8,128)(2,1)} fusion(bf16[24,128,256]{2,1,0:T(8,128)(2,1)} %bitcast.7, s32[1024]{0:T(1024)S(1)} %pad_clamp_fusion.1), kind=kCustom, calls=%fused_computation.2 | custom fusion | bytes 3145824 | tf_op jit(solution)/shard_map/gather | solution.py:27
  66.8 0.0 copy-start.1
  66.8 3.2 %multiply_convert_fusion = bf16[24,128,128]{2,1,0:T(8,128)(2,1)S(1)} fusion(s32[24,128,128]{2,1,0:T(8,128)} %param.8, bf16[24,128,256]{1,2,0:T(8,128)(2,1)} %gather_fusion, bf16[24,128,256]{2,1,0:T(8,128)(2,1)} %gather_fusion.2, f32[24]{0:T(128)S(1)} %compare_select_fusion.8), kind=kOutput, calls=%fused_computation.10 | convolution fusion | flops 202899456 | bytes 5505120 | tf_op jit(solution)/shard_map/ogj,omj->ogm/dot_general | solution.py:33
  69.9 0.0 copy-done.1
  70.0 1.8 %convolution_convert_fusion = bf16[24,128,256]{2,1,0:T(8,128)(2,1)} fusion(bf16[24,128,128]{2,1,0:T(8,128)(2,1)S(1)} %multiply_convert_fusion, bf16[24,128,256]{1,2,0:T(8,128)(2,1)S(1)} %copy-done.1), kind=kOutput, calls=%fused_computation.5 | convolution fusion | flops 202113024 | bytes 3932160 | tf_op jit(solution)/shard_map/yzj,yzh->yjh/dot_general | solution.py:47
  71.7 3.2 %gather_fusion.4 = bf16[24,128,256]{2,1,0:T(8,128)(2,1)} fusion(bf16[24,128,256]{2,1,0:T(8,128)(2,1)} %convolution_convert_fusion, s32[1024]{0:T(1024)S(1)} %pad_clamp_fusion), kind=kCustom, calls=%fused_computation.4 | custom fusion | bytes 3145824 | tf_op jit(solution)/shard_map/gather | solution.py:50
  75.0 0.0 copy-start.3
  75.0 4.5 %all-to-all-start.1 = ((bf16[4,6,128,256]{3,2,1,0:T(8,128)(2,1)}), bf16[4,6,128,256]{3,2,1,0:T(8,128)(2,1)}, u32[]{:S(2)}, u32[]{:S(2)}) async-start(bf16[4,6,128,256]{3,2,1,0:T(8,128)(2,1)} %bitcast.52), calls=%async_computation.1 | async-start | bytes 3145728 | tf_op jit(solution)/shard_map/all_to_all | solution.py:52
  79.5 0.0 reduce-scatter.2.cloned.1.call-start
  79.5 0.0 copy-done.3
  79.5 0.1 eq.19
  79.6 36.6 %all-to-all-done.1 = bf16[4,6,128,256]{3,2,1,0:T(8,128)(2,1)} async-done(((bf16[4,6,128,256]{3,2,1,0:T(8,128)(2,1)}), bf16[4,6,128,256]{3,2,1,0:T(8,128)(2,1)}, u32[]{:S(2)}, u32[]{:S(2)}) %all-to-all-start.1) | async-done | bytes 1572896 | tf_op jit(solution)/shard_map/all_to_all | solution.py:52
  116.2 2.6 %fusion = f32[8,128,256]{2,0,1:T(8,128)S(1)} fusion(s32[24]{0:T(128)S(1)} %eq.19, bf16[3,8,128,256]{3,2,1,0:T(8,128)(2,1)} %bitcast.19), kind=kOutput, calls=%fused_computation.7 | convolution fusion | flops 12583104 | bytes 2621536 | tf_op jit(solution)/shard_map/dot_general | solution.py:59
  118.8 1.3 copy.17
  120.2 0.0 reduce-scatter.2.cloned.1.call-update
  120.2 2.5 %gather_fusion.3 = bf16[24,256,256]{2,1,0:T(8,128)(2,1)} fusion(bf16[16,256,256]{2,1,0:T(8,128)(2,1)S(1)} %copy-done, s32[1024]{0:T(1024)S(1)} %pad_clamp_fusion.3), kind=kCustom, calls=%fused_computation.3 | custom fusion | bytes 6291552 | tf_op jit(solution)/shard_map/gather | solution.py:43
  122.7 31.8 %reduce-scatter.2.cloned.1.call-done = f32[1,128,256]{2,1,0:T(8,128)} async-done(((f32[8,128,256]{2,1,0:T(8,128)}), f32[1,128,256]{2,1,0:T(8,128)}) %reduce-scatter.2.cloned.1.call-update) | async-done | bytes 131088 | tf_op jit(solution)/shard_map/reduce_scatter | solution.py:65
  154.5 4.6 %fusion.6 = f32[128,256]{1,0:T(8,128)} fusion(bf16[24,256,256]{2,1,0:T(8,128)(2,1)} %gather_fusion.3, bf16[24,128,128]{2,1,0:T(8,128)(2,1)S(1)} %multiply_convert_fusion, bf16[24,128,256]{2,1,0:T(8,128)(2,1)} %gather_fusion.2, f32[1,128,256]{2,1,0:T(8,128)} %reduce-scatter.2.cloned.1.call-done), kind=kOutput, calls=%fused_computation.15 | convolution fusion | flops 604798976 | bytes 5767168 | tf_op jit(solution)/shard_map/tbs,trs->br/dot_general | solution.py:42
  (9 shorter events, 0.1 us)
Async XLA Ops:
  6.5 20.1 %copy-start = (bf16[16,256,256]{2,1,0:T(8,128)(2,1)S(1)}, bf16[16,256,256]{2,1,0:T(8,128)(2,1)}, u32[]{:S(2)}) copy-start(bf16[16,256,256]{2,1,0:T(8,128)(2,1)} %param.7) | copy-start | bytes 6291460
  20.9 5.7 %copy-start.4 = (s32[1,24]{1,0:T(1,128)S(1)}, s32[1,24]{1,0:T(1,128)}, u32[]{:S(2)}) copy-start(s32[1,24]{1,0:T(1,128)} %param.9) | copy-start | bytes 292
  20.9 5.7 %copy-start.2 = (bf16[128,256]{1,0:T(8,128)(2,1)S(1)}, bf16[128,256]{1,0:T(8,128)(2,1)}, u32[]{:S(2)}) copy-start(bf16[128,256]{1,0:T(8,128)(2,1)} %param.6) | copy-start | bytes 196612
  20.9 42.6 %all-to-all-start = ((bf16[4,6,128,256]{3,2,1,0:T(8,128)(2,1)}), bf16[4,6,128,256]{3,2,1,0:T(8,128)(2,1)}, u32[]{:S(2)}, u32[]{:S(2)}) async-start(bf16[4,6,128,256]{3,2,1,0:T(8,128)(2,1)} %bitcast.51), calls=%async_computation | async-start | bytes 3145728 | tf_op jit(solution)/shard_map/all_to_all | solution.py:22
  66.8 3.2 %copy-start.1 = (bf16[24,128,256]{1,2,0:T(8,128)(2,1)S(1)}, bf16[24,128,256]{1,2,0:T(8,128)(2,1)}, u32[]{:S(2)}) copy-start(bf16[24,128,256]{1,2,0:T(8,128)(2,1)} %gather_fusion) | copy-start | bytes 4718596
  75.0 4.5 %copy-start.3 = (s32[1,4,6]{2,1,0:T(4,128)S(1)}, s32[1,4,6]{2,1,0:T(4,128)}, u32[]{:S(2)}) copy-start(s32[1,4,6]{2,1,0:T(4,128)} %param.11) | copy-start | bytes 292
  75.0 41.2 %all-to-all-start.1 = ((bf16[4,6,128,256]{3,2,1,0:T(8,128)(2,1)}), bf16[4,6,128,256]{3,2,1,0:T(8,128)(2,1)}, u32[]{:S(2)}, u32[]{:S(2)}) async-start(bf16[4,6,128,256]{3,2,1,0:T(8,128)(2,1)} %bitcast.52), calls=%async_computation.1 | async-start | bytes 3145728 | tf_op jit(solution)/shard_map/all_to_all | solution.py:52
  79.5 75.0 %reduce-scatter.2.cloned.1.call-start = ((), (), s32[]{:S(2)}) async-start(), calls=%async_computation.3 | async-start | bytes 1179648 | tf_op jit(solution)/shard_map/reduce_scatter | solution.py:65
Sparse Core Ops, SparseCore 0:
  120.3 34.1 reduce-scatter.1
where the time goes:
time: 166 us
  waiting for transfers between devices  103 us (62%)
  local copies, waits for them, and re-layouts  15.2 us (9%)
  between operations  14.2 us (9%)
  matrix products  12.9 us (8%)
  blocking collectives  11.6 us (7%)
  starting transfers between devices  9.52 us (6%)
    all_to_all x1, waiting for transfers between devices, on_device(): lax.all_to_all(sent_terms, 'ent', split_axis=0, concat_axis=0, tiled=True)  36.6 us
    all_to_all x1, waiting for transfers between devices, on_device(): lax.all_to_all(outgoing, 'ent', split_axis=0, concat_axis=0, tiled=True)  34.1 us
    reduce_scatter x1, waiting for transfers between devices, on_device(): lax.psum_scatter(owner_terms.reshape(grp_count, block, width), 'grp', sca...  31.8 us
    all_gather x1, blocking collectives, on_device(): group_blocks = lax.all_gather(factor[None], 'grp', axis=0, tiled=True)  11.6 us
    all_to_all x1, starting transfers between devices, on_device(): lax.all_to_all(outgoing, 'ent', split_axis=0, concat_axis=0, tiled=True)  5 us
    dot_general x1, matrix products, on_device(): jnp.einsum('tbs,trs->br', relation_product, cores[relations], preferred_e...  4.58 us
    all_to_all x1, starting transfers between devices, on_device(): lax.all_to_all(sent_terms, 'ent', split_axis=0, concat_axis=0, tiled=True)  4.48 us
  transfers between devices with their start and end apart: 3, of which 3 were waited for; matrix products, arithmetic and copies ran while one was open for 3% of the time, Pallas kernels for 0%

commit v1 on v0

--- a/solution.py
+++ b/solution.py
@@ -17,7 +17,14 @@
     slots = ent_count * per_relay
     relations = tile_rels[0]
     routes = send_lists[0].reshape(slots)
-    group_blocks = lax.all_gather(factor[None], "grp", axis=0, tiled=True)
+    ways, here, step = (lax.axis_size("grp"), lax.axis_index("grp"), factor[None].shape[0])
+    line, have = (factor[None], 1)
+    while have < ways:
+        line = jnp.concatenate(
+            [line, lax.ppermute(line, "grp", [(d, (d - have) % ways) for d in range(ways)])], axis=0
+        )
+        have = 2 * have
+    group_blocks = jnp.roll(line, here * step, axis=0)
     outgoing = group_blocks[routes].reshape(ent_count, per_relay, block, width)
     arrived = lax.all_to_all(outgoing, "ent", split_axis=0, concat_axis=0, tiled=True).reshape(
         slots, block, width

time: 166 us -> 180 us (1.084)
  blocking collectives: 11.6 us -> 0 us
  waiting for transfers between devices: 103 us -> 113 us
  local copies, waits for them, and re-layouts: 15.2 us -> 22.2 us
  starting transfers between devices: 9.52 us -> 14.6 us
    all_gather x1 -> x0, blocking collectives: 11.6 us -> none  [on_device(): group_blocks = lax.all_gather(factor[None], 'grp', axis=0, tiled=True)]
    ppermute x0 -> x3, waiting for transfers between devices: none -> 10.3 us  [on_device(): lax.ppermute(line, 'grp', [(d, (d - have) % ways) for d in range(ways)])]
    unnamed x10 -> x17, local copies, waits for them, and re-layouts: 0.02 us -> 5.42 us
    ppermute x0 -> x3, starting transfers between devices: none -> 5.11 us  [on_device(): lax.ppermute(line, 'grp', [(d, (d - have) % ways) for d in range(ways)])]
    reduce_scatter x1, waiting for transfers between devices: 31.8 us -> 34.5 us  [on_device(): lax.psum_scatter(owner_terms.reshape(grp_count, block, width), 'grp', sca...]
    all_to_all x1, waiting for transfers between devices: 34.1 us -> 32.3 us  [on_device(): lax.all_to_all(outgoing, 'ent', split_axis=0, concat_axis=0, tiled=True)]
  transfers between devices with their start and end apart: 3 -> 6, of which waited for: 3 -> 5; matrix products, arithmetic and copies ran while one was open for 3% -> 5% of each run, Pallas kernels for 0% -> 0%
where the time goes in v1:
time: 180 us; the launch traced here: 179 us
  waiting for transfers between devices  113 us (63%)
  local copies, waits for them, and re-layouts  22.2 us (12%)
  starting transfers between devices  14.6 us (8%)
  between operations  14.2 us (8%)
  matrix products  12.9 us (7%)
    all_to_all x1, waiting for transfers between devices, on_device(): lax.all_to_all(sent_terms, 'ent', split_axis=0, concat_axis=0, tiled=True)  36.4 us
    reduce_scatter x1, waiting for transfers between devices, on_device(): lax.psum_scatter(owner_terms.reshape(grp_count, block, width), 'grp', sca...  34.5 us
    all_to_all x1, waiting for transfers between devices, on_device(): lax.all_to_all(outgoing, 'ent', split_axis=0, concat_axis=0, tiled=True)  32.3 us
    ppermute x3, waiting for transfers between devices, on_device(): lax.ppermute(line, 'grp', [(d, (d - have) % ways) for d in range(ways)])  10.3 us
    unnamed x17, local copies, waits for them, and re-layouts  5.42 us
    ppermute x3, starting transfers between devices, on_device(): lax.ppermute(line, 'grp', [(d, (d - have) % ways) for d in range(ways)])  5.11 us
    all_to_all x1, starting transfers between devices, on_device(): lax.all_to_all(outgoing, 'ent', split_axis=0, concat_axis=0, tiled=True)  5 us
    dot_general x1, matrix products, on_device(): jnp.einsum('tbs,trs->br', relation_product, cores[relations], preferred_e...  4.59 us
  transfers between devices with their start and end apart: 6, of which 5 were waited for; matrix products, arithmetic and copies ran while one was open for 5% of the time, Pallas kernels for 0%

profile of v1, /device:TPU:0, one launch (start us, length us, event | category | flops | bytes accessed | tf_op | source)
XLA Modules:
  0.0 179.1 jit_solution(15211434512584239237)
XLA Ops:
  6.5 0.0 copy-start
  6.5 0.0 copy-start.2
  6.5 3.3 %collective-permute-start = (bf16[1,128,256]{2,1,0:T(8,128)(2,1)}, bf16[1,128,256]{2,1,0:T(8,128)(2,1)S(1)}, u32[]{:S(2)}, u32[]{:S(2)}) collective-permute-start(bf16[1,128,256]{2,1,0:T(8,128)(2,1)} %bitcast.54), channel_id=1, source_target_pairs={{0,28},{4,0},{8,4},{12,8},{16,12},{20,16},{24,20},{28,24},{1,29},{... | collective-permute-start | bytes 196616 | tf_op jit(solution)/shard_map/ppermute | solution.py:24
  9.9 1.5 constant_dynamic-update-slice_fusion.7
  11.4 0.8 reshape_squeeze.3
  12.1 0.0 collective-permute-done
  12.1 0.9 pad_maximum_fusion.1
  13.0 0.7 collective-permute-start.1
  13.7 4.9 %collective-permute-done.1 = bf16[2,128,256]{2,1,0:T(8,128)(2,1)S(1)} collective-permute-done((bf16[2,128,256]{2,1,0:T(8,128)(2,1)S(1)}, bf16[2,128,256]{2,1,0:T(8,128)(2,1)S(1)}, u32[]{:S(2)}, u32[]{:S(2)}) %collective-permute-start.1) | collective-permute-done | bytes 131104 | tf_op jit(solution)/shard_map/ppermute | solution.py:24
  18.7 0.9 pad_maximum_fusion
  19.6 1.0 collective-permute-start.2
  20.6 0.6 constant_dynamic-update-slice_fusion.6
  21.2 0.7 constant_dynamic-update-slice_fusion.5
  21.9 5.4 %collective-permute-done.2 = bf16[4,128,256]{2,1,0:T(8,128)(2,1)S(1)} collective-permute-done((bf16[4,128,256]{2,1,0:T(8,128)(2,1)S(1)}, bf16[4,128,256]{2,1,0:T(8,128)(2,1)S(1)}, u32[]{:S(2)}, u32[]{:S(2)}) %collective-permute-start.2) | collective-permute-done | bytes 262176 | tf_op jit(solution)/shard_map/ppermute | solution.py:24
  27.2 0.7 constant_dynamic-update-slice_fusion.4
  28.0 0.0 copy-done.2
  28.0 0.6 constant_dynamic-update-slice_fusion.3
  28.6 0.6 constant_dynamic-update-slice_fusion.2
  29.2 0.7 constant_dynamic-update-slice_fusion.1
  29.9 0.7 constant_dynamic-update-slice_fusion
  30.6 1.1 constant_dynamic-slice_fusion
  31.7 1.9 %gather_fusion.1 = bf16[24,128,256]{2,1,0:T(8,128)(2,1)} fusion(bf16[8,128,256]{2,1,0:T(8,128)(2,1)S(1)} %constant_dynamic-slice_fusion, s32[1024]{0:T(1024)S(1)} %pad_clamp_fusion.2), kind=kCustom, calls=%fused_computation.1 | custom fusion | bytes 3145824 | tf_op jit(solution)/shard_map/gather | solution.py:28
  33.5 0.0 copy-start.4
  33.5 5.0 %all-to-all-start = ((bf16[4,6,128,256]{3,2,1,0:T(8,128)(2,1)}), bf16[4,6,128,256]{3,2,1,0:T(8,128)(2,1)}, u32[]{:S(2)}, u32[]{:S(2)}) async-start(bf16[4,6,128,256]{3,2,1,0:T(8,128)(2,1)} %bitcast.52), calls=%async_computation | async-start | bytes 3145728 | tf_op jit(solution)/shard_map/all_to_all | solution.py:29
  39.2 0.0 copy-done.4
  39.2 0.0 copy-done
  39.3 0.8 fusion.4
  40.0 1.9 %gather_fusion = bf16[24,128,256]{1,2,0:T(8,128)(2,1)} fusion(bf16[16,128,256]{1,2,0:T(8,128)(2,1)S(1)} %fusion.4, s32[1024]{0:T(1024)S(1)} %get-tuple-element.6), kind=kCustom, calls=%fused_computation | custom fusion | bytes 3145824 | tf_op jit(solution)/shard_map/gather | solution.py:39
  42.0 32.3 %all-to-all-done = bf16[4,6,128,256]{3,2,1,0:T(8,128)(2,1)} async-done(((bf16[4,6,128,256]{3,2,1,0:T(8,128)(2,1)}), bf16[4,6,128,256]{3,2,1,0:T(8,128)(2,1)}, u32[]{:S(2)}, u32[]{:S(2)}) %all-to-all-start) | async-done | bytes 1572896 | tf_op jit(solution)/shard_map/all_to_all | solution.py:29
  74.3 3.3 %gather_fusion.2 = bf16[24,128,256]{2,1,0:T(8,128)(2,1)} fusion(bf16[24,128,256]{2,1,0:T(8,128)(2,1)} %bitcast.7, s32[1024]{0:T(1024)S(1)} %get-tuple-element.5), kind=kCustom, calls=%fused_computation.2 | custom fusion | bytes 3145824 | tf_op jit(solution)/shard_map/gather | solution.py:34
  77.5 0.0 copy-start.1
  77.5 3.2 %multiply_convert_fusion = bf16[24,128,128]{2,1,0:T(8,128)(2,1)S(1)} fusion(s32[24,128,128]{2,1,0:T(8,128)} %param.8, bf16[24,128,256]{1,2,0:T(8,128)(2,1)} %gather_fusion, bf16[24,128,256]{2,1,0:T(8,128)(2,1)} %gather_fusion.2, f32[24]{0:T(128)S(1)} %compare_select_fusion.8), kind=kOutput, calls=%fused_computation.10 | convolution fusion | flops 202899456 | bytes 5505120 | tf_op jit(solution)/shard_map/ogj,omj->ogm/dot_general | solution.py:40
  80.7 0.0 copy-done.1
  80.7 1.8 convolution_convert_fusion
  82.5 3.3 %gather_fusion.4 = bf16[24,128,256]{2,1,0:T(8,128)(2,1)} fusion(bf16[24,128,256]{2,1,0:T(8,128)(2,1)} %convolution_convert_fusion, s32[1024]{0:T(1024)S(1)} %pad_clamp_fusion), kind=kCustom, calls=%fused_computation.4 | custom fusion | bytes 3145824 | tf_op jit(solution)/shard_map/gather | solution.py:57
  85.8 0.0 copy-start.3
  85.8 4.5 %all-to-all-start.1 = ((bf16[4,6,128,256]{3,2,1,0:T(8,128)(2,1)}), bf16[4,6,128,256]{3,2,1,0:T(8,128)(2,1)}, u32[]{:S(2)}, u32[]{:S(2)}) async-start(bf16[4,6,128,256]{3,2,1,0:T(8,128)(2,1)} %bitcast.53), calls=%async_computation.1 | async-start | bytes 3145728 | tf_op jit(solution)/shard_map/all_to_all | solution.py:59
  90.2 0.0 reduce-scatter.2.cloned.1.call-start
  90.3 0.0 copy-done.3
  90.3 0.1 eq.22
  90.4 36.4 %all-to-all-done.1 = bf16[4,6,128,256]{3,2,1,0:T(8,128)(2,1)} async-done(((bf16[4,6,128,256]{3,2,1,0:T(8,128)(2,1)}), bf16[4,6,128,256]{3,2,1,0:T(8,128)(2,1)}, u32[]{:S(2)}, u32[]{:S(2)}) %all-to-all-start.1) | async-done | bytes 1572896 | tf_op jit(solution)/shard_map/all_to_all | solution.py:59
  126.7 2.6 %fusion = f32[8,128,256]{2,0,1:T(8,128)S(1)} fusion(s32[24]{0:T(128)S(1)} %eq.22, bf16[3,8,128,256]{3,2,1,0:T(8,128)(2,1)} %bitcast.19), kind=kOutput, calls=%fused_computation.7 | convolution fusion | flops 12583104 | bytes 2621536 | tf_op jit(solution)/shard_map/dot_general | solution.py:66
  129.4 1.3 copy.17
  130.7 0.0 reduce-scatter.2.cloned.1.call-update
  130.7 2.5 %gather_fusion.3 = bf16[24,256,256]{2,1,0:T(8,128)(2,1)} fusion(bf16[16,256,256]{2,1,0:T(8,128)(2,1)S(1)} %copy-done, s32[1024]{0:T(1024)S(1)} %get-tuple-element.6), kind=kCustom, calls=%fused_computation.3 | custom fusion | bytes 6291552 | tf_op jit(solution)/shard_map/gather | solution.py:50
  133.2 34.5 %reduce-scatter.2.cloned.1.call-done = f32[1,128,256]{2,1,0:T(8,128)} async-done(((f32[8,128,256]{2,1,0:T(8,128)}), f32[1,128,256]{2,1,0:T(8,128)}) %reduce-scatter.2.cloned.1.call-update) | async-done | bytes 131088 | tf_op jit(solution)/shard_map/reduce_scatter | solution.py:72
  167.7 4.6 %fusion.6 = f32[128,256]{1,0:T(8,128)} fusion(bf16[24,256,256]{2,1,0:T(8,128)(2,1)} %gather_fusion.3, bf16[24,128,128]{2,1,0:T(8,128)(2,1)S(1)} %multiply_convert_fusion, bf16[24,128,256]{2,1,0:T(8,128)(2,1)} %gather_fusion.2, f32[1,128,256]{2,1,0:T(8,128)} %reduce-scatter.2.cloned.1.call-done), kind=kOutput, calls=%fused_computation.15 | convolution fusion | flops 604798976 | bytes 5767168 | tf_op jit(solution)/shard_map/tbs,trs->br/dot_general | solution.py:49
  (8 shorter events, 0.1 us)
Async XLA Ops:
  6.5 32.7 %copy-start = (bf16[16,256,256]{2,1,0:T(8,128)(2,1)S(1)}, bf16[16,256,256]{2,1,0:T(8,128)(2,1)}, u32[]{:S(2)}) copy-start(bf16[16,256,256]{2,1,0:T(8,128)(2,1)} %param.7) | copy-start | bytes 6291460
  6.5 21.4 %copy-start.2 = (bf16[128,256]{1,0:T(8,128)(2,1)S(1)}, bf16[128,256]{1,0:T(8,128)(2,1)}, u32[]{:S(2)}) copy-start(bf16[128,256]{1,0:T(8,128)(2,1)} %param.6) | copy-start | bytes 196612
  6.5 5.6 %collective-permute-start = (bf16[1,128,256]{2,1,0:T(8,128)(2,1)}, bf16[1,128,256]{2,1,0:T(8,128)(2,1)S(1)}, u32[]{:S(2)}, u32[]{:S(2)}) collective-permute-start(bf16[1,128,256]{2,1,0:T(8,128)(2,1)} %bitcast.54), channel_id=1, source_target_pairs={{0,28},{4,0},{8,4},{12,8},{16,12},{20,16},{24,20},{28,24},{1,29},{... | collective-permute-start | bytes 196616 | tf_op jit(solution)/shard_map/ppermute | solution.py:24
  13.0 5.7 %collective-permute-start.1 = (bf16[2,128,256]{2,1,0:T(8,128)(2,1)S(1)}, bf16[2,128,256]{2,1,0:T(8,128)(2,1)S(1)}, u32[]{:S(2)}, u32[]{:S(2)}) collective-permute-start(bf16[2,128,256]{2,1,0:T(8,128)(2,1)S(1)} %pad_maximum_fusion.1), channel_id=1, source_target_pairs={{0,24},{4,28},{8,0},{12,4},{16,8},{20,12},{24,16},{28,20},{1,25},{... | collective-permute-start | bytes 393224 | tf_op jit(solution)/shard_map/ppermute | solution.py:24
  19.6 7.7 %collective-permute-start.2 = (bf16[4,128,256]{2,1,0:T(8,128)(2,1)S(1)}, bf16[4,128,256]{2,1,0:T(8,128)(2,1)S(1)}, u32[]{:S(2)}, u32[]{:S(2)}) collective-permute-start(bf16[4,128,256]{2,1,0:T(8,128)(2,1)S(1)} %pad_maximum_fusion), channel_id=1, source_target_pairs={{0,16},{4,20},{8,24},{12,28},{16,0},{20,4},{24,8},{28,12},{1,17},{... | collective-permute-start | bytes 786440 | tf_op jit(solution)/shard_map/ppermute | solution.py:24
  33.5 5.7 %copy-start.4 = (s32[1,24]{1,0:T(1,128)S(1)}, s32[1,24]{1,0:T(1,128)}, u32[]{:S(2)}) copy-start(s32[1,24]{1,0:T(1,128)} %param.9) | copy-start | bytes 292
  33.5 40.7 %all-to-all-start = ((bf16[4,6,128,256]{3,2,1,0:T(8,128)(2,1)}), bf16[4,6,128,256]{3,2,1,0:T(8,128)(2,1)}, u32[]{:S(2)}, u32[]{:S(2)}) async-start(bf16[4,6,128,256]{3,2,1,0:T(8,128)(2,1)} %bitcast.52), calls=%async_computation | async-start | bytes 3145728 | tf_op jit(solution)/shard_map/all_to_all | solution.py:29
  77.5 3.2 %copy-start.1 = (bf16[24,128,256]{1,2,0:T(8,128)(2,1)S(1)}, bf16[24,128,256]{1,2,0:T(8,128)(2,1)}, u32[]{:S(2)}) copy-start(bf16[24,128,256]{1,2,0:T(8,128)(2,1)} %gather_fusion) | copy-start | bytes 4718596
  85.8 4.5 %copy-start.3 = (s32[1,4,6]{2,1,0:T(4,128)S(1)}, s32[1,4,6]{2,1,0:T(4,128)}, u32[]{:S(2)}) copy-start(s32[1,4,6]{2,1,0:T(4,128)} %param.11) | copy-start | bytes 292
  85.8 41.0 %all-to-all-start.1 = ((bf16[4,6,128,256]{3,2,1,0:T(8,128)(2,1)}), bf16[4,6,128,256]{3,2,1,0:T(8,128)(2,1)}, u32[]{:S(2)}, u32[]{:S(2)}) async-start(bf16[4,6,128,256]{3,2,1,0:T(8,128)(2,1)} %bitcast.53), calls=%async_computation.1 | async-start | bytes 3145728 | tf_op jit(solution)/shard_map/all_to_all | solution.py:59
  90.2 77.4 %reduce-scatter.2.cloned.1.call-start = ((), (), s32[]{:S(2)}) async-start(), calls=%async_computation.3 | async-start | bytes 1179648 | tf_op jit(solution)/shard_map/reduce_scatter | solution.py:72
Sparse Core Ops, SparseCore 0:
  130.9 36.7 reduce-scatter.1
